TPU v7x, 32 devices: a whole 2x2x4 slice. The times are simulated.
32 devices in a mesh: seq: 4 (over y, x), shard: 8 (over z, core).
Axes of the slice: x: 2, y: 2, z: 4, core: 2. Of those that a mesh axis runs over, the one named last changes fastest.
Arguments:
- layer_in: bfloat16 [32, 1024, 768], P('shard', 'seq'), may hold values from -6 to 6
- layer_cotangent: bfloat16 [32, 1024, 768], P('shard', 'seq'), may hold values from -6 to 6
- doc_starts: int32 [32, 17], P('shard'), may hold values from 0 to 1024, as said below
- query_weight: float32 [768, 768], P(('seq', 'shard')), may hold values from -0.21875 to 0.21875
- key_weight: float32 [768, 768], P(('seq', 'shard')), may hold values from -0.21875 to 0.21875
- value_weight: float32 [768, 768], P(('seq', 'shard')), may hold values from -0.21875 to 0.21875
- out_weight: float32 [768, 768], P(('seq', 'shard')), may hold values from -3.5 to 3.5
- up_weight: float32 [768, 3072], P(('seq', 'shard')), may hold values from -0.21875 to 0.21875
- down_weight: float32 [3072, 768], P(('seq', 'shard')), may hold values from -0.109375 to 0.109375
- query_bias: float32 [768], P(('seq', 'shard')), may hold values from -0.625 to 0.625
- value_bias: float32 [768], P(('seq', 'shard')), may hold values from -0.1875 to 0.1875
- out_bias: float32 [768], P(('seq', 'shard')), may hold values from -0.625 to 0.625
- up_bias: float32 [3072], P(('seq', 'shard')), may hold values from -0.625 to 0.625
- down_bias: float32 [768], P(('seq', 'shard')), may hold values from -0.625 to 0.625
- mixer_gain: float32 [768], P(('seq', 'shard')), may hold values from 0.5 to 1.5
- mixer_shift: float32 [768], P(('seq', 'shard')), may hold values from -0.625 to 0.625
- final_gain: float32 [768], P(('seq', 'shard')), may hold values from 0.5 to 1.5
- final_shift: float32 [768], P(('seq', 'shard')), may hold values from -0.625 to 0.625
Outputs:
- layer_out: bfloat16 [32, 1024, 768], P('shard', 'seq')
- input_grad: float32 [32, 1024, 768], P('shard', 'seq')
- grad_query_weight: float32 [768, 768], P(('seq', 'shard'))
- grad_key_weight: float32 [768, 768], P(('seq', 'shard'))
- grad_value_weight: float32 [768, 768], P(('seq', 'shard'))
- grad_out_weight: float32 [768, 768], P(('seq', 'shard'))
- grad_up_weight: float32 [768, 3072], P(('seq', 'shard'))
- grad_down_weight: float32 [3072, 768], P(('seq', 'shard'))
- grad_query_bias: float32 [768], P(('seq', 'shard'))
- grad_value_bias: float32 [768], P(('seq', 'shard'))
- grad_out_bias: float32 [768], P(('seq', 'shard'))
- grad_up_bias: float32 [3072], P(('seq', 'shard'))
- grad_down_bias: float32 [768], P(('seq', 'shard'))
- grad_mixer_gain: float32 [768], P(('seq', 'shard'))
- grad_mixer_shift: float32 [768], P(('seq', 'shard'))
- grad_final_gain: float32 [768], P(('seq', 'shard'))
- grad_final_shift: float32 [768], P(('seq', 'shard'))
Inputs may be any that keep to these rules, and one draw needn't show every extreme that they name: `doc_starts`: each row lists the first positions of the documents of its stream in rising order; it begins with 0, entries equal to 1024 mark unused slots, and the last entry is always 1024. A document spans at most 512 positions, some document of every stream exactly that; every document but the last of a stream spans at least 64.
All inputs are finite; a program needn't handle non-finite values.
Results may differ from a plain program's by a relative error of at most 0.017.
Values may be sent and summed in bfloat16 or wider, within the bound.
No kernel may reach another device: no remote copies, remote signals or barrier semaphores. Data moves between devices by JAX's collectives and lax.ppermute only.
A program may use at most 192 MiB of HBM per device.

v0:
```python
import jax
import jax.numpy as jnp
from jax import lax
from jax.sharding import PartitionSpec as P

DH = 64
LEN = 1024
EPS = 1e-06
NEG = -1e30
ROOT_HALF = 0.7071067811865476
INV_ROOT_TWO_PI = 0.3989422804014327


def contract_rows(left, right):
    return lax.dot_general(
        left, right, (((0,), (0,)), ((), ())), preferred_element_type=jnp.float32
    )


def times_transpose(left, right):
    return lax.dot_general(
        left, right, (((1,), (1,)), ((), ())), preferred_element_type=jnp.float32
    )


def segment_ids(starts, length):
    places = lax.broadcasted_iota(jnp.int32, (1, length, 1), 1)
    return jnp.sum((starts[:, None, :] <= places).astype(jnp.int32), axis=2)


def norm_forward(rows, gain, shift):
    middle = jnp.mean(rows, axis=-1, keepdims=True)
    centred = rows - middle
    spread = jnp.mean(centred * centred, axis=-1, keepdims=True)
    inverse = lax.rsqrt(spread + EPS)
    normed = centred * inverse
    return (normed * gain + shift, normed, inverse)


def norm_backward(upstream, gain, normed, inverse):
    scaled = upstream * gain
    inner = jnp.mean(scaled, axis=-1, keepdims=True)
    along = jnp.mean(scaled * normed, axis=-1, keepdims=True)
    return inverse * (scaled - inner - normed * along)


def gelu_value(value):
    return 0.5 * value * (1.0 + lax.erf(value * ROOT_HALF))


def gelu_slope(value):
    return (
        0.5 * (1.0 + lax.erf(value * ROOT_HALF))
        + value * jnp.exp(-0.5 * value * value) * INV_ROOT_TWO_PI
    )


def masked_scores(queries, keys, seg_rows, seg_all, scale):
    scores = jnp.einsum("qhd,khd->hqk", queries, keys, preferred_element_type=jnp.float32) * scale
    allowed = seg_rows[:, None] == seg_all[None, :]
    return jnp.where(allowed[None], scores, NEG)


def attend_forward(item):
    queries, keys, values, segment = item
    length, heads, depth = queries.shape
    rows = min(512, length)
    blocks = length // rows
    scale = depth ** (-0.5)

    def one(piece):
        block_q, block_seg = piece
        scores = masked_scores(block_q, keys, block_seg, segment, scale)
        highest = jnp.max(scores, axis=-1, keepdims=True)
        raised = jnp.exp(scores - highest)
        total = jnp.sum(raised, axis=-1, keepdims=True)
        weights = (raised / total).astype(jnp.bfloat16)
        context = jnp.einsum("hqk,khd->qhd", weights, values, preferred_element_type=jnp.float32)
        return (context.astype(jnp.bfloat16), (highest + jnp.log(total))[..., 0])

    context, logsum = lax.map(
        one, (queries.reshape(blocks, rows, heads, depth), segment.reshape(blocks, rows))
    )
    return (context.reshape(length, heads, depth), logsum)


def attend_backward(item):
    queries, keys, values, segment, logsum, upstream = item
    length, heads, depth = queries.shape
    rows = min(512, length)
    blocks = length // rows
    scale = depth ** (-0.5)

    def one(carry, piece):
        key_acc, value_acc = carry
        block_q, block_seg, block_sum, block_up = piece
        scores = masked_scores(block_q, keys, block_seg, segment, scale)
        weights = jnp.exp(scores - block_sum[..., None])
        value_acc = value_acc + jnp.einsum(
            "hqk,qhd->khd",
            weights.astype(jnp.bfloat16),
            block_up,
            preferred_element_type=jnp.float32,
        )
        slope = jnp.einsum("qhd,khd->hqk", block_up, values, preferred_element_type=jnp.float32)
        inner = jnp.sum(weights * slope, axis=-1, keepdims=True)
        score_grad = (weights * (slope - inner)).astype(jnp.bfloat16)
        query_grad = (
            jnp.einsum("hqk,khd->qhd", score_grad, keys, preferred_element_type=jnp.float32) * scale
        )
        key_acc = (
            key_acc
            + jnp.einsum("hqk,qhd->khd", score_grad, block_q, preferred_element_type=jnp.float32)
            * scale
        )
        return ((key_acc, value_acc), query_grad.astype(jnp.bfloat16))

    empty = jnp.zeros((length, heads, depth), jnp.float32)
    pieces = (
        queries.reshape(blocks, rows, heads, depth),
        segment.reshape(blocks, rows),
        logsum,
        upstream.reshape(blocks, rows, heads, depth),
    )
    (key_grad, value_grad), query_grad = lax.scan(one, (empty, empty), pieces)
    return (
        query_grad.reshape(length, heads, depth),
        key_grad.astype(jnp.bfloat16),
        value_grad.astype(jnp.bfloat16),
    )


def per_device(
    layer_in,
    layer_cotangent,
    doc_starts,
    query_weight,
    key_weight,
    value_weight,
    out_weight,
    up_weight,
    down_weight,
    query_bias,
    value_bias,
    out_bias,
    up_bias,
    down_bias,
    mixer_gain,
    mixer_shift,
    final_gain,
    final_shift,
):
    (
        full_query,
        full_key,
        full_value,
        full_out,
        full_up,
        full_down,
        bias_query,
        bias_value,
        bias_out,
        bias_up,
        bias_down,
        gain_mixer,
        shift_mixer,
        gain_final,
        shift_final,
    ) = (
        lax.all_gather(query_weight.astype(jnp.bfloat16), ("seq", "shard"), axis=0, tiled=True),
        lax.all_gather(key_weight.astype(jnp.bfloat16), ("seq", "shard"), axis=0, tiled=True),
        lax.all_gather(value_weight.astype(jnp.bfloat16), ("seq", "shard"), axis=0, tiled=True),
        lax.all_gather(out_weight.astype(jnp.bfloat16), ("seq", "shard"), axis=0, tiled=True),
        lax.all_gather(up_weight.astype(jnp.bfloat16), ("seq", "shard"), axis=0, tiled=True),
        lax.all_gather(down_weight.astype(jnp.bfloat16), ("seq", "shard"), axis=0, tiled=True),
        lax.all_gather(query_bias.astype(jnp.bfloat16), ("seq", "shard"), axis=0, tiled=True),
        lax.all_gather(value_bias.astype(jnp.bfloat16), ("seq", "shard"), axis=0, tiled=True),
        lax.all_gather(out_bias.astype(jnp.bfloat16), ("seq", "shard"), axis=0, tiled=True),
        lax.all_gather(up_bias.astype(jnp.bfloat16), ("seq", "shard"), axis=0, tiled=True),
        lax.all_gather(down_bias.astype(jnp.bfloat16), ("seq", "shard"), axis=0, tiled=True),
        lax.all_gather(mixer_gain.astype(jnp.bfloat16), ("seq", "shard"), axis=0, tiled=True),
        lax.all_gather(mixer_shift.astype(jnp.bfloat16), ("seq", "shard"), axis=0, tiled=True),
        lax.all_gather(final_gain.astype(jnp.bfloat16), ("seq", "shard"), axis=0, tiled=True),
        lax.all_gather(final_shift.astype(jnp.bfloat16), ("seq", "shard"), axis=0, tiled=True),
    )
    local_in, local_up = (layer_in, layer_cotangent)
    streams, part_len, width = local_in.shape
    row_count = streams * part_len
    heads = width // DH
    flat = local_in.reshape(row_count, width)
    split_shape = (streams, part_len, heads, DH)
    queries = (
        jnp.dot(flat, full_query, preferred_element_type=jnp.float32)
        + bias_query.astype(jnp.float32)
    ).astype(jnp.bfloat16)
    keys = jnp.dot(flat, full_key, preferred_element_type=jnp.float32).astype(jnp.bfloat16)
    values = (
        jnp.dot(flat, full_value, preferred_element_type=jnp.float32)
        + bias_value.astype(jnp.float32)
    ).astype(jnp.bfloat16)
    head_queries, head_keys, head_values = (
        lax.all_to_all(
            queries.reshape(split_shape), "seq", split_axis=2, concat_axis=1, tiled=True
        ),
        lax.all_to_all(keys.reshape(split_shape), "seq", split_axis=2, concat_axis=1, tiled=True),
        lax.all_to_all(values.reshape(split_shape), "seq", split_axis=2, concat_axis=1, tiled=True),
    )
    segment = segment_ids(doc_starts, LEN)
    context, logsum = lax.map(attend_forward, (head_queries, head_keys, head_values, segment))
    context_rows = lax.all_to_all(context, "seq", split_axis=1, concat_axis=2, tiled=True).reshape(
        row_count, width
    )
    attn = jnp.dot(context_rows, full_out, preferred_element_type=jnp.float32) + bias_out.astype(
        jnp.float32
    )
    mixed, normed_mixer, inverse_mixer = norm_forward(
        flat.astype(jnp.float32) + attn,
        gain_mixer.astype(jnp.float32),
        shift_mixer.astype(jnp.float32),
    )
    upper = mixed.astype(jnp.bfloat16)
    preact = jnp.dot(upper, full_up, preferred_element_type=jnp.float32) + bias_up.astype(
        jnp.float32
    )
    hidden = gelu_value(preact).astype(jnp.bfloat16)
    ffout = jnp.dot(hidden, full_down, preferred_element_type=jnp.float32) + bias_down.astype(
        jnp.float32
    )
    result, normed_final, inverse_final = norm_forward(
        mixed + ffout, gain_final.astype(jnp.float32), shift_final.astype(jnp.float32)
    )
    layer_out = result.astype(jnp.bfloat16).reshape(streams, part_len, width)
    upstream = local_up.reshape(row_count, width).astype(jnp.float32)
    grad_final_gain = jnp.sum(upstream * normed_final, axis=0)
    grad_final_shift = jnp.sum(upstream, axis=0)
    back_final = norm_backward(
        upstream, gain_final.astype(jnp.float32), normed_final, inverse_final
    )
    back_ffout = back_final.astype(jnp.bfloat16)
    grad_down_weight = contract_rows(hidden, back_ffout)
    grad_down_bias = jnp.sum(back_ffout.astype(jnp.float32), axis=0)
    back_preact = (times_transpose(back_ffout, full_down) * gelu_slope(preact)).astype(jnp.bfloat16)
    grad_up_weight = contract_rows(upper, back_preact)
    grad_up_bias = jnp.sum(back_preact.astype(jnp.float32), axis=0)
    back_mixed = back_final + times_transpose(back_preact, full_up)
    grad_mixer_gain = jnp.sum(back_mixed * normed_mixer, axis=0)
    grad_mixer_shift = jnp.sum(back_mixed, axis=0)
    back_first = norm_backward(
        back_mixed, gain_mixer.astype(jnp.float32), normed_mixer, inverse_mixer
    )
    back_attn = back_first.astype(jnp.bfloat16)
    grad_out_weight = contract_rows(context_rows, back_attn)
    grad_out_bias = jnp.sum(back_attn.astype(jnp.float32), axis=0)
    back_context = times_transpose(back_attn, full_out).astype(jnp.bfloat16)
    head_back = lax.all_to_all(
        back_context.reshape(split_shape), "seq", split_axis=2, concat_axis=1, tiled=True
    )
    query_back, key_back, value_back = lax.map(
        attend_backward, (head_queries, head_keys, head_values, segment, logsum, head_back)
    )
    query_rows, key_rows, value_rows = (
        lax.all_to_all(query_back, "seq", split_axis=1, concat_axis=2, tiled=True),
        lax.all_to_all(key_back, "seq", split_axis=1, concat_axis=2, tiled=True),
        lax.all_to_all(value_back, "seq", split_axis=1, concat_axis=2, tiled=True),
    )
    query_rows = query_rows.reshape(row_count, width)
    key_rows = key_rows.reshape(row_count, width)
    value_rows = value_rows.reshape(row_count, width)
    grad_query_weight = contract_rows(flat, query_rows)
    grad_key_weight = contract_rows(flat, key_rows)
    grad_value_weight = contract_rows(flat, value_rows)
    grad_query_bias = jnp.sum(query_rows.astype(jnp.float32), axis=0)
    grad_value_bias = jnp.sum(value_rows.astype(jnp.float32), axis=0)
    input_grad = (
        back_first
        + times_transpose(query_rows, full_query)
        + times_transpose(key_rows, full_key)
        + times_transpose(value_rows, full_value)
    ).reshape(streams, part_len, width)
    (
        sum_query_weight,
        sum_key_weight,
        sum_value_weight,
        sum_out_weight,
        sum_up_weight,
        sum_down_weight,
        sum_query_bias,
        sum_value_bias,
        sum_out_bias,
        sum_up_bias,
        sum_down_bias,
        sum_mixer_gain,
        sum_mixer_shift,
        sum_final_gain,
        sum_final_shift,
    ) = (
        lax.psum_scatter(grad_query_weight, ("seq", "shard"), scatter_dimension=0, tiled=True),
        lax.psum_scatter(grad_key_weight, ("seq", "shard"), scatter_dimension=0, tiled=True),
        lax.psum_scatter(grad_value_weight, ("seq", "shard"), scatter_dimension=0, tiled=True),
        lax.psum_scatter(grad_out_weight, ("seq", "shard"), scatter_dimension=0, tiled=True),
        lax.psum_scatter(grad_up_weight, ("seq", "shard"), scatter_dimension=0, tiled=True),
        lax.psum_scatter(grad_down_weight, ("seq", "shard"), scatter_dimension=0, tiled=True),
        lax.psum_scatter(grad_query_bias, ("seq", "shard"), scatter_dimension=0, tiled=True),
        lax.psum_scatter(grad_value_bias, ("seq", "shard"), scatter_dimension=0, tiled=True),
        lax.psum_scatter(grad_out_bias, ("seq", "shard"), scatter_dimension=0, tiled=True),
        lax.psum_scatter(grad_up_bias, ("seq", "shard"), scatter_dimension=0, tiled=True),
        lax.psum_scatter(grad_down_bias, ("seq", "shard"), scatter_dimension=0, tiled=True),
        lax.psum_scatter(grad_mixer_gain, ("seq", "shard"), scatter_dimension=0, tiled=True),
        lax.psum_scatter(grad_mixer_shift, ("seq", "shard"), scatter_dimension=0, tiled=True),
        lax.psum_scatter(grad_final_gain, ("seq", "shard"), scatter_dimension=0, tiled=True),
        lax.psum_scatter(grad_final_shift, ("seq", "shard"), scatter_dimension=0, tiled=True),
    )
    return (
        layer_out,
        input_grad,
        sum_query_weight,
        sum_key_weight,
        sum_value_weight,
        sum_out_weight,
        sum_up_weight,
        sum_down_weight,
        sum_query_bias,
        sum_value_bias,
        sum_out_bias,
        sum_up_bias,
        sum_down_bias,
        sum_mixer_gain,
        sum_mixer_shift,
        sum_final_gain,
        sum_final_shift,
    )


def solution(mesh):
    in_specs = (
        P("shard", "seq", None),
        P("shard", "seq", None),
        P("shard", None),
        P(("seq", "shard"), None),
        P(("seq", "shard"), None),
        P(("seq", "shard"), None),
        P(("seq", "shard"), None),
        P(("seq", "shard"), None),
        P(("seq", "shard"), None),
        P(("seq", "shard")),
        P(("seq", "shard")),
        P(("seq", "shard")),
        P(("seq", "shard")),
        P(("seq", "shard")),
        P(("seq", "shard")),
        P(("seq", "shard")),
        P(("seq", "shard")),
        P(("seq", "shard")),
    )
    out_specs = (
        P("shard", "seq", None),
        P("shard", "seq", None),
        P(("seq", "shard"), None),
        P(("seq", "shard"), None),
        P(("seq", "shard"), None),
        P(("seq", "shard"), None),
        P(("seq", "shard"), None),
        P(("seq", "shard"), None),
        P(("seq", "shard")),
        P(("seq", "shard")),
        P(("seq", "shard")),
        P(("seq", "shard")),
        P(("seq", "shard")),
        P(("seq", "shard")),
        P(("seq", "shard")),
        P(("seq", "shard")),
        P(("seq", "shard")),
    )
    return jax.shard_map(
        per_device, mesh=mesh, in_specs=in_specs, out_specs=out_specs, check_vma=False
    )
```

profile of v0, /device:TPU:0, one launch (start us, length us, event | category | flops | bytes accessed | tf_op | source)
XLA Modules:
  0.0 1251.4 jit_solution(2350865984096955184)
XLA Ops:
  23.0 42.7 %all-reduce.19 = (bf16[768]{0:T(1024)(128)(2,1)S(1)}, bf16[768]{0:T(1024)(128)(2,1)S(1)}, bf16[768]{0:T(1024)(128)(2,1)}, bf16[768]{0:T(1024)(128)(2,1)}, bf16[7...) all-reduce(bf16[768]{0:T(1024)(128)(2,1)S(1)} %dynamic-update-slice, ...), channel_id=1, replica_groups=mesh['seq'=4,'shard'=8] {'seq','shard'}, use_global_device_ids=true, to_apply=%add | all-reduce | flops 9216 | bytes 36864
  78.3 52.2 %all-gather.7.cloned.1.call-done = bf16[768,768]{1,0:T(8,128)(2,1)} async-done(((bf16[24,768]{1,0:T(8,128)(2,1)}), bf16[768,768]{1,0:T(8,128)(2,1)}) %all-gather.7.cloned.1.call-update) | async-done | bytes 1179664 | tf_op jit(solution)/shard_map/all_gather | solution.py:170
  142.5 49.7 %all-gather.9.cloned.1.call-done = bf16[768,768]{1,0:T(8,128)(2,1)} async-done(((bf16[24,768]{1,0:T(8,128)(2,1)}), bf16[768,768]{1,0:T(8,128)(2,1)}) %all-gather.9.cloned.1.call-update) | async-done | bytes 1179664 | tf_op jit(solution)/shard_map/all_gather | solution.py:171
  211.3 17.1 %all-to-all-done.1 = bf16[4,256,12,64]{1,0,3,2:T(4,128)(2,1)} async-done(((bf16[4,256,12,64]{1,0,3,2:T(4,128)(2,1)}), bf16[4,256,12,64]{1,0,3,2:T(4,128)(2,1)}, u32[]{:S(2)}, u32[]{:S(2)}) %all-to-all-start.1) | async-done | bytes 1572896 | tf_op jit(solution)/shard_map/all_to_all | solution.py:205
  234.5 70.0 %while.54 = (s32[]{:T(128)}, bf16[4,1024,3,64]{3,2,1,0:T(4,128)(2,1)}, f32[4,2,3,512]{3,2,1,0:T(4,128)}, bf16[4,1024,3,64]{1,3,2,0:T(8,128)(2,1)S(1)}, s32[4,102...) while((s32[]{:T(128)}, ...), condition=%wide.region_6.7_spmd, body=%wide.region_1.6_spmd.sunk | while | flops 422148608 | bytes 28430672 | solution.py:209
  290.5 11.3 while.57
  324.4 18.5 %all-to-all-done.3 = bf16[4,2,98304]{2,1,0:T(2,128)(2,1)} async-done(((bf16[4,2,98304]{2,1,0:T(2,128)(2,1)}), bf16[4,2,98304]{2,1,0:T(2,128)(2,1)}, u32[]{:S(2)}, u32[]{:S(2)}) %all-to-all-start.3) | async-done | bytes 1572896 | tf_op jit(solution)/shard_map/all_to_all | solution.py:210
  357.9 12.8 %multiply_convert_fusion.1 = (bf16[1024,3072]{1,0:T(8,128)(2,1)}, f32[1024,3072]{1,0:T(8,128)}) fusion(f32[3072]{0:T(1024)S(1)} %convert_element_type.186, bf16[768,3072]{1,0:T(8,128)(2,1)} %all-gather.15.cloned.1.call-done, f32[1024,768]{1,0:T(8,128)S(1)} %get-tuple-element.625, f32[768]{0:T(1024)S(1)} %convert_element_type.182, ...), kind=kOutput, calls=%fused_computation.75 | convolution fusion | flops 4854644736 | bytes 26765312 | tf_op jit(solution)/shard_map/dot_general | solution.py:222
  370.7 14.1 %all-gather.17.cloned.1.call-done = bf16[3072,768]{1,0:T(8,128)(2,1)} async-done(((bf16[96,768]{1,0:T(8,128)(2,1)}), bf16[3072,768]{1,0:T(8,128)(2,1)}) %all-gather.17.cloned.1.call-update) | async-done | bytes 4718608 | tf_op jit(solution)/shard_map/all_gather | solution.py:175
  399.7 14.1 %convert_reduce_fusion = (f32[3072]{0:T(1024)}, bf16[1024,3072]{1,0:T(8,128)(2,1)S(1)}) fusion(f32[1024,3072]{1,0:T(8,128)} %get-tuple-element.627, f32[3072]{0:T(1024)S(1)} %convert_element_type.186, bf16[3072,768]{1,0:T(8,128)(2,1)S(1)} %copy-done.46, f32[1024,768]{1,0:T(8,128)S(1)} %get-tuple-element.612), kind=kOutput, calls=%fused_computation.74 | convolution fusion | flops 4873516032 | bytes 26763264 | tf_op jit(solution)/shard_map/dot_general | solution.py:21
  439.7 15.6 %all-to-all-done.4 = bf16[4,256,12,64]{1,0,3,2:T(4,128)(2,1)} async-done(((bf16[4,256,12,64]{1,0,3,2:T(4,128)(2,1)}), bf16[4,256,12,64]{1,0,3,2:T(4,128)(2,1)}, u32[]{:S(2)}, u32[]{:S(2)}) %all-to-all-start.4) | async-done | bytes 1572896 | tf_op jit(solution)/shard_map/all_to_all | solution.py:255
  461.4 142.2 %while.56 = (s32[]{:T(128)}, bf16[4,1024,3,64]{3,2,1,0:T(4,128)(2,1)}, bf16[4,1024,3,64]{1,3,2,0:T(8,128)(2,1)}, bf16[4,1024,3,64]{1,3,2,0:T(8,128)(2,1)}, bf16[...) while((s32[]{:T(128)}, ...), condition=%wide.region_19.20_spmd, body=%wide.region_15.19_spmd.sunk | while | flops 1032321536 | bytes 67146216 | solution.py:258
  470.3 22.2 %while.58 = (s32[]{:T(128)}, f32[1024,3,64]{0,2,1:T(8,128)S(1)}, f32[1024,3,64]{0,2,1:T(8,128)S(1)}, bf16[2,512,3,64]{1,3,2,0:T(8,128)(2,1)S(1)}, bf16[2,512,3,6...) while((s32[]{:T(128)}, f32[1024,3,64]{0,2,1:T(8,128)S(1)}, ...), condition=%wide.region_18.18_spmd.clone, body=%wide.region_16.17_spmd.clone.sunk | while | flops 1031928320 | bytes 54649000 | solution.py:125
  505.8 22.2 %while.58 = (s32[]{:T(128)}, f32[1024,3,64]{0,2,1:T(8,128)S(1)}, f32[1024,3,64]{0,2,1:T(8,128)S(1)}, bf16[2,512,3,64]{1,3,2,0:T(8,128)(2,1)S(1)}, bf16[2,512,3,6...) while((s32[]{:T(128)}, f32[1024,3,64]{0,2,1:T(8,128)S(1)}, ...), condition=%wide.region_18.18_spmd.clone, body=%wide.region_16.17_spmd.clone.sunk | while | flops 1031928320 | bytes 54649000 | solution.py:125
  541.3 22.2 %while.58 = (s32[]{:T(128)}, f32[1024,3,64]{0,2,1:T(8,128)S(1)}, f32[1024,3,64]{0,2,1:T(8,128)S(1)}, bf16[2,512,3,64]{1,3,2,0:T(8,128)(2,1)S(1)}, bf16[2,512,3,6...) while((s32[]{:T(128)}, f32[1024,3,64]{0,2,1:T(8,128)S(1)}, ...), condition=%wide.region_18.18_spmd.clone, body=%wide.region_16.17_spmd.clone.sunk | while | flops 1031928320 | bytes 54649000 | solution.py:125
  576.8 22.2 %while.58 = (s32[]{:T(128)}, f32[1024,3,64]{0,2,1:T(8,128)S(1)}, f32[1024,3,64]{0,2,1:T(8,128)S(1)}, bf16[2,512,3,64]{1,3,2,0:T(8,128)(2,1)S(1)}, bf16[2,512,3,6...) while((s32[]{:T(128)}, f32[1024,3,64]{0,2,1:T(8,128)S(1)}, ...), condition=%wide.region_18.18_spmd.clone, body=%wide.region_16.17_spmd.clone.sunk | while | flops 1031928320 | bytes 54649000 | solution.py:125
  611.7 23.3 %all_to_all.132 = bf16[4,2,98304]{2,1,0:T(2,128)(2,1)S(1)} all-to-all(bf16[4,2,98304]{2,1,0:T(2,128)(2,1)} %reshape.306), channel_id=1, replica_groups=mesh['seq'=4,'shard'=8] {'seq'}, dimensions={0} | all-to-all | bytes 3145728 | tf_op jit(solution)/shard_map/all_to_all | solution.py:264
  660.5 21.9 %all_to_all.133 = bf16[4,2,98304]{2,1,0:T(2,128)(2,1)S(1)} all-to-all(bf16[4,2,98304]{2,1,0:T(2,128)(2,1)} %reshape.304), channel_id=1, replica_groups=mesh['seq'=4,'shard'=8] {'seq'}, dimensions={0} | all-to-all | bytes 3145728 | tf_op jit(solution)/shard_map/all_to_all | solution.py:262
  706.3 23.6 %all_to_all.134 = bf16[4,2,98304]{2,1,0:T(2,128)(2,1)} all-to-all(bf16[4,2,98304]{2,1,0:T(2,128)(2,1)} %reshape.302), channel_id=1, replica_groups=mesh['seq'=4,'shard'=8] {'seq'}, dimensions={0} | all-to-all | bytes 3145728 | tf_op jit(solution)/shard_map/all_to_all | solution.py:263
  774.7 40.4 %all-reduce.18 = (f32[768]{0:T(1024)S(1)}, f32[768]{0:T(1024)S(1)}, f32[768]{0:T(1024)S(1)}, f32[3072]{0:T(1024)S(1)}, f32[768]{0:T(1024)S(1)}, /*index=5*/f32[7...) all-reduce(f32[768]{0:T(1024)S(1)} %reduce_sum.194, ...), channel_id=8, replica_groups=mesh['seq'=4,'shard'=8] {'seq','shard'}, use_global_device_ids=true, to_apply=%region_27.28.clone | all-reduce | flops 9216 | bytes 73728
  829.7 27.2 %reduce-scatter.19.cloned.1.call-done = f32[24,768]{1,0:T(8,128)} async-done(((f32[768,768]{1,0:T(8,128)}), f32[24,768]{1,0:T(8,128)}) %reduce-scatter.19.cloned.1.call-update) | async-done | bytes 73744
  856.9 104.3 %reduce-scatter.21.cloned.1.call-done = f32[24,768]{1,0:T(8,128)} async-done(((f32[768,768]{1,0:T(8,128)}), f32[24,768]{1,0:T(8,128)}) %reduce-scatter.21.cloned.1.call-update) | async-done | bytes 73744
  961.2 141.7 %reduce-scatter.15.cloned.1.call-done = f32[24,3072]{1,0:T(8,128)} async-done(((f32[768,3072]{1,0:T(8,128)}), f32[24,3072]{1,0:T(8,128)}) %reduce-scatter.15.cloned.1.call-update) | async-done | bytes 294928 | tf_op jit(solution)/shard_map/reduce_scatter | solution.py:301
  1102.9 141.5 %reduce-scatter.17.cloned.1.call-done = f32[96,768]{1,0:T(8,128)} async-done(((f32[3072,768]{1,0:T(8,128)}), f32[96,768]{1,0:T(8,128)}) %reduce-scatter.17.cloned.1.call-update) | async-done | bytes 294928 | tf_op jit(solution)/shard_map/reduce_scatter | solution.py:302
  (525 shorter events, 507.9 us)
Async XLA Ops:
  7.2 61.3 %all-gather.11.cloned.1.call-start = ((), (), s32[]{:S(2)}) async-start(), calls=%async_computation.16 | async-start | bytes 1216512 | tf_op jit(solution)/shard_map/all_gather | solution.py:172
  8.8 121.8 %all-gather.7.cloned.1.call-start = ((), (), s32[]{:S(2)}) async-start(), calls=%async_computation.14 | async-start | bytes 1216512 | tf_op jit(solution)/shard_map/all_gather | solution.py:170
  10.3 181.8 %all-gather.9.cloned.1.call-start = ((), (), s32[]{:S(2)}) async-start(), calls=%async_computation.15 | async-start | bytes 1216512 | tf_op jit(solution)/shard_map/all_gather | solution.py:171
  11.9 341.5 %all-gather.13.cloned.1.call-start = ((), (), s32[]{:S(2)}) async-start(), calls=%async_computation.17 | async-start | bytes 1216512 | tf_op jit(solution)/shard_map/all_gather | solution.py:173
  13.5 344.4 %all-gather.15.cloned.1.call-start = ((), (), s32[]{:S(2)}) async-start(), calls=%async_computation.18 | async-start | bytes 4866048 | tf_op jit(solution)/shard_map/all_gather | solution.py:174
  74.7 64.2 %all-to-all-start.2 = ((bf16[4,256,12,64]{1,0,3,2:T(4,128)(2,1)}), bf16[4,256,12,64]{1,0,3,2:T(4,128)(2,1)S(1)}, u32[]{:S(2)}, u32[]{:S(2)}) async-start(bf16[4,256,12,64]{1,0,3,2:T(4,128)(2,1)} %reshape.249), calls=%async_computation.2 | async-start | bytes 3145728 | tf_op jit(solution)/shard_map/all_to_all | solution.py:206
  138.9 64.1 %all-to-all-start = ((bf16[4,256,12,64]{1,0,3,2:T(4,128)(2,1)}), bf16[4,256,12,64]{1,0,3,2:T(4,128)(2,1)S(1)}, u32[]{:S(2)}, u32[]{:S(2)}) async-start(bf16[4,256,12,64]{1,0,3,2:T(4,128)(2,1)} %reshape.247), calls=%async_computation | async-start | bytes 3145728 | tf_op jit(solution)/shard_map/all_to_all | solution.py:202
  203.0 25.4 %all-to-all-start.1 = ((bf16[4,256,12,64]{1,0,3,2:T(4,128)(2,1)}), bf16[4,256,12,64]{1,0,3,2:T(4,128)(2,1)}, u32[]{:S(2)}, u32[]{:S(2)}) async-start(bf16[4,256,12,64]{1,0,3,2:T(4,128)(2,1)} %reshape.248), calls=%async_computation.1 | async-start | bytes 3145728 | tf_op jit(solution)/shard_map/all_to_all | solution.py:205
  207.3 177.4 %all-gather.17.cloned.1.call-start = ((), (), s32[]{:S(2)}) async-start(), calls=%async_computation.19 | async-start | bytes 4866048 | tf_op jit(solution)/shard_map/all_gather | solution.py:175
  318.2 24.7 %all-to-all-start.3 = ((bf16[4,2,98304]{2,1,0:T(2,128)(2,1)}), bf16[4,2,98304]{2,1,0:T(2,128)(2,1)}, u32[]{:S(2)}, u32[]{:S(2)}) async-start(bf16[4,2,98304]{2,1,0:T(2,128)(2,1)} %reshape.300), calls=%async_computation.3 | async-start | bytes 3145728 | tf_op jit(solution)/shard_map/all_to_all | solution.py:210
  322.9 97.4 %copy-start.27 = (f32[768]{0:T(1024)}, f32[768]{0:T(1024)S(1)}, u32[]{:S(2)}) copy-start(f32[768]{0:T(1024)S(1)} %convert_element_type.180) | copy-start | bytes 9220
  323.0 61.8 %copy-start.29 = (f32[768]{0:T(1024)}, f32[768]{0:T(1024)S(1)}, u32[]{:S(2)}) copy-start(f32[768]{0:T(1024)S(1)} %convert_element_type.182) | copy-start | bytes 9220
  357.3 63.0 %copy-start = (f32[1024,768]{1,0:T(8,128)}, f32[1024,768]{1,0:T(8,128)S(1)}, u32[]{:S(2)}) copy-start(f32[1024,768]{1,0:T(8,128)S(1)} %get-tuple-element.625) | copy-start | bytes 9437188
  357.3 63.0 %copy-start.22 = (f32[1024]{0:T(1024)}, f32[1024]{0:T(1024)S(1)}, u32[]{:S(2)}) copy-start(f32[1024]{0:T(1024)S(1)} %broadcast_multiply_fusion.4) | copy-start | bytes 12292
  357.9 62.5 %copy-start.25 = (f32[1024]{0:T(1024)}, f32[1024]{0:T(1024)S(1)}, u32[]{:S(2)}) copy-start(f32[1024]{0:T(1024)S(1)} %add_rsqrt_fusion.1) | copy-start | bytes 12292
  396.8 17.0 %slice-start = ((s8[4718592]{0:T(1024)(128)(4,1)}), s8[4194304]{0:T(1024)(128)(4,1)S(1)}, s32[]{:S(2)}) async-start(s8[4718592]{0:T(1024)(128)(4,1)} %bitcast.311), calls=%async_computation.26 | async-start | bytes 8388608
  399.7 14.1 %copy-start.16 = (f32[1024,768]{1,0:T(8,128)}, f32[1024,768]{1,0:T(8,128)S(1)}, u32[]{:S(2)}) copy-start(f32[1024,768]{1,0:T(8,128)S(1)} %get-tuple-element.612) | copy-start | bytes 9437188
  430.9 24.4 %all-to-all-start.4 = ((bf16[4,256,12,64]{1,0,3,2:T(4,128)(2,1)}), bf16[4,256,12,64]{1,0,3,2:T(4,128)(2,1)}, u32[]{:S(2)}, u32[]{:S(2)}) async-start(bf16[4,256,12,64]{1,0,3,2:T(4,128)(2,1)} %reshape.252), calls=%async_computation.4 | async-start | bytes 3145728 | tf_op jit(solution)/shard_map/all_to_all | solution.py:255
  435.3 394.4 %reduce-scatter.13.cloned.1.call-start = ((), (), s32[]{:S(2)}) async-start(), calls=%async_computation.20 | async-start | bytes 2433024 | tf_op jit(solution)/shard_map/reduce_scatter | solution.py:300
  439.6 390.1 %reduce-scatter.23.cloned.1.call-start = ((), (), s32[]{:S(2)}) async-start(), calls=%async_computation.25 | async-start | bytes 2433024
  650.9 206.0 %reduce-scatter.19.cloned.1.call-start = ((), (), s32[]{:S(2)}) async-start(), calls=%async_computation.23 | async-start | bytes 2433024
  698.2 263.0 %reduce-scatter.21.cloned.1.call-start = ((), (), s32[]{:S(2)}) async-start(), calls=%async_computation.24 | async-start | bytes 2433024
  746.6 356.3 %reduce-scatter.15.cloned.1.call-start = ((), (), s32[]{:S(2)}) async-start(), calls=%async_computation.21 | async-start | bytes 9732096 | tf_op jit(solution)/shard_map/reduce_scatter | solution.py:301
  757.5 486.9 %reduce-scatter.17.cloned.1.call-start = ((), (), s32[]{:S(2)}) async-start(), calls=%async_computation.22 | async-start | bytes 9732096 | tf_op jit(solution)/shard_map/reduce_scatter | solution.py:302
  (50 other events, 245.6 us)
Sparse Core Ops, SparseCore 0:
  11.6 56.8 all-gather.10
  72.0 58.4 all-gather.6
  134.2 57.9 all-gather.8
  195.6 53.8 all-gather.12
  252.9 62.5 all-gather.14
  318.9 65.7 all-gather.16
  442.0 99.3 reduce-scatter.12
  651.0 101.0 reduce-scatter.22
  758.0 98.8 reduce-scatter.18
  862.6 98.5 reduce-scatter.20
  967.7 135.1 reduce-scatter.14
  1109.2 135.0 reduce-scatter.16
where the time goes:
time: 1260 us; the launch traced here: 1250 us
  waiting for transfers between devices  585 us (46%)
  local copies, waits for them, and re-layouts  217 us (17%)
  matrix products  188 us (15%)
  blocking collectives  152 us (12%)
  other arithmetic  71.6 us (6%)
  starting transfers between devices  21.2 us (2%)
  between operations  15.3 us (1%)
    reduce_scatter x1, waiting for transfers between devices, per_device(): lax.psum_scatter(grad_up_weight, ('seq', 'shard'), scatter_dimension=0, t...  142 us
    reduce_scatter x1, waiting for transfers between devices, per_device(): lax.psum_scatter(grad_down_weight, ('seq', 'shard'), scatter_dimension=0,...  141 us
    unnamed x15, waiting for transfers between devices  132 us
    unnamed x2, blocking collectives  83.1 us
    unnamed x150, local copies, waits for them, and re-layouts  62.4 us
    all_gather x1, waiting for transfers between devices, per_device(): lax.all_gather(query_weight.astype(jnp.bfloat16), ('seq', 'shard'), axis=...  52.2 us
    all_gather x1, waiting for transfers between devices, per_device(): lax.all_gather(key_weight.astype(jnp.bfloat16), ('seq', 'shard'), axis=0,...  49.7 us
    dot_general x6, matrix products, contract_rows(): lax.dot_general(left, right, (((0,), (0,)), ((), ())), preferred_element_...  33.5 us
  transfers between devices with their start and end apart: 17, of which 11 were waited for; matrix products, arithmetic and copies ran while one was open for 33% of the time, Pallas kernels for 0%

commit v1 on v0

--- a/solution.py
+++ b/solution.py
@@ -258,9 +258,18 @@
     query_back, key_back, value_back = lax.map(
         attend_backward, (head_queries, head_keys, head_values, segment, logsum, head_back)
     )
+
+    def handle_the_lane(buf, along_axis):
+        w_next = lax.axis_size(along_axis)
+        t1 = jnp.split(buf, w_next, axis=1)
+        near = jnp.stack(t1)
+        state_now = lax.all_to_all(near, along_axis, 0, 0)
+        outer = jnp.concatenate(state_now, axis=2)
+        return outer
+
     query_rows, key_rows, value_rows = (
         lax.all_to_all(query_back, "seq", split_axis=1, concat_axis=2, tiled=True),
-        lax.all_to_all(key_back, "seq", split_axis=1, concat_axis=2, tiled=True),
+        handle_the_lane(key_back, "seq"),
         lax.all_to_all(value_back, "seq", split_axis=1, concat_axis=2, tiled=True),
     )
     query_rows = query_rows.reshape(row_count, width)

time: 1260 us -> 1250 us (level)
  local copies, waits for them, and re-layouts: 217 us -> 201 us
    unnamed x150 -> x148, local copies, waits for them, and re-layouts: 62.4 us -> 52.6 us
  transfers between devices with their start and end apart: 17 -> 17, of which waited for: 11 -> 11; matrix products, arithmetic and copies ran while one was open for 33% -> 32% of each run, Pallas kernels for 0% -> 0%
where the time goes in v1:
time: 1250 us; the launch traced here: 1230 us
  waiting for transfers between devices  587 us (47%)
  local copies, waits for them, and re-layouts  201 us (16%)
  matrix products  187 us (15%)
  blocking collectives  150 us (12%)
  other arithmetic  71.9 us (6%)
  starting transfers between devices  21.2 us (2%)
  between operations  15.3 us (1%)
    reduce_scatter x1, waiting for transfers between devices, per_device(): lax.psum_scatter(grad_up_weight, ('seq', 'shard'), scatter_dimension=0, t...  142 us
    reduce_scatter x1, waiting for transfers between devices, per_device(): lax.psum_scatter(grad_down_weight, ('seq', 'shard'), scatter_dimension=0,...  141 us
    unnamed x15, waiting for transfers between devices  134 us
    unnamed x2, blocking collectives  82.8 us
    unnamed x148, local copies, waits for them, and re-layouts  52.6 us
    all_gather x1, waiting for transfers between devices, per_device(): lax.all_gather(query_weight.astype(jnp.bfloat16), ('seq', 'shard'), axis=...  52.2 us
    all_gather x1, waiting for transfers between devices, per_device(): lax.all_gather(key_weight.astype(jnp.bfloat16), ('seq', 'shard'), axis=0,...  49.7 us
    dot_general x6, matrix products, contract_rows(): lax.dot_general(left, right, (((0,), (0,)), ((), ())), preferred_element_...  32.2 us
  transfers between devices with their start and end apart: 17, of which 11 were waited for; matrix products, arithmetic and copies ran while one was open for 32% of the time, Pallas kernels for 0%

profile of v1, /device:TPU:0, one launch (start us, length us, event | category | flops | bytes accessed | tf_op | source)
XLA Modules:
  0.0 1234.3 jit_solution(17089423095850186009)
XLA Ops:
  23.0 42.7 %all-reduce.19 = (bf16[768]{0:T(1024)(128)(2,1)S(1)}, bf16[768]{0:T(1024)(128)(2,1)S(1)}, bf16[768]{0:T(1024)(128)(2,1)}, bf16[768]{0:T(1024)(128)(2,1)}, bf16[7...) all-reduce(bf16[768]{0:T(1024)(128)(2,1)S(1)} %dynamic-update-slice, ...), channel_id=1, replica_groups=mesh['seq'=4,'shard'=8] {'seq','shard'}, use_global_device_ids=true, to_apply=%add | all-reduce | flops 9216 | bytes 36864
  78.3 52.2 %all-gather.7.cloned.1.call-done = bf16[768,768]{1,0:T(8,128)(2,1)} async-done(((bf16[24,768]{1,0:T(8,128)(2,1)}), bf16[768,768]{1,0:T(8,128)(2,1)}) %all-gather.7.cloned.1.call-update) | async-done | bytes 1179664 | tf_op jit(solution)/shard_map/all_gather | solution.py:170
  142.5 49.7 %all-gather.9.cloned.1.call-done = bf16[768,768]{1,0:T(8,128)(2,1)} async-done(((bf16[24,768]{1,0:T(8,128)(2,1)}), bf16[768,768]{1,0:T(8,128)(2,1)}) %all-gather.9.cloned.1.call-update) | async-done | bytes 1179664 | tf_op jit(solution)/shard_map/all_gather | solution.py:171
  211.3 17.1 %all-to-all-done.1 = bf16[4,256,12,64]{1,0,3,2:T(4,128)(2,1)} async-done(((bf16[4,256,12,64]{1,0,3,2:T(4,128)(2,1)}), bf16[4,256,12,64]{1,0,3,2:T(4,128)(2,1)}, u32[]{:S(2)}, u32[]{:S(2)}) %all-to-all-start.1) | async-done | bytes 1572896 | tf_op jit(solution)/shard_map/all_to_all | solution.py:205
  234.5 70.0 %while.54 = (s32[]{:T(128)}, bf16[4,1024,3,64]{3,2,1,0:T(4,128)(2,1)}, f32[4,2,3,512]{3,2,1,0:T(4,128)}, bf16[4,1024,3,64]{1,3,2,0:T(8,128)(2,1)S(1)}, s32[4,102...) while((s32[]{:T(128)}, ...), condition=%wide.region_6.7_spmd, body=%wide.region_1.6_spmd.sunk | while | flops 422148608 | bytes 28430672 | solution.py:209
  238.0 11.3 while.57
  324.4 18.5 %all-to-all-done.3 = bf16[4,2,98304]{2,1,0:T(2,128)(2,1)} async-done(((bf16[4,2,98304]{2,1,0:T(2,128)(2,1)}), bf16[4,2,98304]{2,1,0:T(2,128)(2,1)}, u32[]{:S(2)}, u32[]{:S(2)}) %all-to-all-start.3) | async-done | bytes 1572896 | tf_op jit(solution)/shard_map/all_to_all | solution.py:210
  357.9 12.7 %multiply_convert_fusion.1 = (bf16[1024,3072]{1,0:T(8,128)(2,1)}, f32[1024,3072]{1,0:T(8,128)}) fusion(f32[3072]{0:T(1024)S(1)} %convert_element_type.186, bf16[768,3072]{1,0:T(8,128)(2,1)} %all-gather.15.cloned.1.call-done, f32[1024,768]{1,0:T(8,128)S(1)} %get-tuple-element.629, f32[768]{0:T(1024)S(1)} %convert_element_type.182, ...), kind=kOutput, calls=%fused_computation.75 | convolution fusion | flops 4854644736 | bytes 26765312 | tf_op jit(solution)/shard_map/dot_general | solution.py:222
  370.6 14.1 %all-gather.17.cloned.1.call-done = bf16[3072,768]{1,0:T(8,128)(2,1)} async-done(((bf16[96,768]{1,0:T(8,128)(2,1)}), bf16[3072,768]{1,0:T(8,128)(2,1)}) %all-gather.17.cloned.1.call-update) | async-done | bytes 4718608 | tf_op jit(solution)/shard_map/all_gather | solution.py:175
  399.7 14.1 %convert_reduce_fusion = (f32[3072]{0:T(1024)}, bf16[1024,3072]{1,0:T(8,128)(2,1)S(1)}) fusion(f32[1024,3072]{1,0:T(8,128)} %get-tuple-element.631, f32[3072]{0:T(1024)S(1)} %convert_element_type.186, bf16[3072,768]{1,0:T(8,128)(2,1)S(1)} %copy-done.46, f32[1024,768]{1,0:T(8,128)S(1)} %get-tuple-element.612), kind=kOutput, calls=%fused_computation.74 | convolution fusion | flops 4873516032 | bytes 26763264 | tf_op jit(solution)/shard_map/dot_general | solution.py:21
  439.7 15.6 %all-to-all-done.4 = bf16[4,256,12,64]{1,0,3,2:T(4,128)(2,1)} async-done(((bf16[4,256,12,64]{1,0,3,2:T(4,128)(2,1)}), bf16[4,256,12,64]{1,0,3,2:T(4,128)(2,1)}, u32[]{:S(2)}, u32[]{:S(2)}) %all-to-all-start.4) | async-done | bytes 1572896 | tf_op jit(solution)/shard_map/all_to_all | solution.py:255
  461.4 142.2 %while.56 = (s32[]{:T(128)}, bf16[4,1024,3,64]{3,2,1,0:T(4,128)(2,1)}, bf16[4,1024,3,64]{1,3,2,0:T(8,128)(2,1)}, bf16[4,1024,3,64]{1,3,2,0:T(8,128)(2,1)}, bf16[...) while((s32[]{:T(128)}, ...), condition=%wide.region_19.20_spmd, body=%wide.region_15.19_spmd.sunk | while | flops 1032321536 | bytes 67146216 | solution.py:258
  470.2 22.2 %while.58 = (s32[]{:T(128)}, f32[1024,3,64]{0,2,1:T(8,128)S(1)}, f32[1024,3,64]{0,2,1:T(8,128)S(1)}, bf16[2,512,3,64]{1,3,2,0:T(8,128)(2,1)S(1)}, bf16[2,512,3,6...) while((s32[]{:T(128)}, f32[1024,3,64]{0,2,1:T(8,128)S(1)}, ...), condition=%wide.region_18.18_spmd.clone, body=%wide.region_16.17_spmd.clone.sunk | while | flops 1031928320 | bytes 54649000 | solution.py:125
  505.7 22.2 %while.58 = (s32[]{:T(128)}, f32[1024,3,64]{0,2,1:T(8,128)S(1)}, f32[1024,3,64]{0,2,1:T(8,128)S(1)}, bf16[2,512,3,64]{1,3,2,0:T(8,128)(2,1)S(1)}, bf16[2,512,3,6...) while((s32[]{:T(128)}, f32[1024,3,64]{0,2,1:T(8,128)S(1)}, ...), condition=%wide.region_18.18_spmd.clone, body=%wide.region_16.17_spmd.clone.sunk | while | flops 1031928320 | bytes 54649000 | solution.py:125
  541.3 22.1 %while.58 = (s32[]{:T(128)}, f32[1024,3,64]{0,2,1:T(8,128)S(1)}, f32[1024,3,64]{0,2,1:T(8,128)S(1)}, bf16[2,512,3,64]{1,3,2,0:T(8,128)(2,1)S(1)}, bf16[2,512,3,6...) while((s32[]{:T(128)}, f32[1024,3,64]{0,2,1:T(8,128)S(1)}, ...), condition=%wide.region_18.18_spmd.clone, body=%wide.region_16.17_spmd.clone.sunk | while | flops 1031928320 | bytes 54649000 | solution.py:125
  576.8 22.1 %while.58 = (s32[]{:T(128)}, f32[1024,3,64]{0,2,1:T(8,128)S(1)}, f32[1024,3,64]{0,2,1:T(8,128)S(1)}, bf16[2,512,3,64]{1,3,2,0:T(8,128)(2,1)S(1)}, bf16[2,512,3,6...) while((s32[]{:T(128)}, f32[1024,3,64]{0,2,1:T(8,128)S(1)}, ...), condition=%wide.region_18.18_spmd.clone, body=%wide.region_16.17_spmd.clone.sunk | while | flops 1031928320 | bytes 54649000 | solution.py:125
  605.4 22.3 %all_to_all.122 = bf16[4,4,256,3,64]{2,4,3,1,0:T(8,128)(2,1)S(1)} all-to-all(bf16[4,4,256,3,64]{2,4,3,1,0:T(8,128)(2,1)S(1)} %pad_maximum_fusion), channel_id=1, replica_groups=mesh['seq'=4,'shard'=8] {'seq'}, dimensions={0} | all-to-all | bytes 3145728 | tf_op jit(solution)/shard_map/all_to_all | solution.py:266
  641.9 21.9 %all_to_all.123 = bf16[4,2,98304]{2,1,0:T(2,128)(2,1)S(1)} all-to-all(bf16[4,2,98304]{2,1,0:T(2,128)(2,1)} %reshape.303), channel_id=1, replica_groups=mesh['seq'=4,'shard'=8] {'seq'}, dimensions={0} | all-to-all | bytes 3145728 | tf_op jit(solution)/shard_map/all_to_all | solution.py:273
  689.2 22.6 %all_to_all.124 = bf16[4,2,98304]{2,1,0:T(2,128)(2,1)S(1)} all-to-all(bf16[4,2,98304]{2,1,0:T(2,128)(2,1)} %reshape.301), channel_id=1, replica_groups=mesh['seq'=4,'shard'=8] {'seq'}, dimensions={0} | all-to-all | bytes 3145728 | tf_op jit(solution)/shard_map/all_to_all | solution.py:271
  755.8 40.1 %all-reduce.18 = (f32[768]{0:T(1024)S(1)}, f32[768]{0:T(1024)S(1)}, f32[768]{0:T(1024)S(1)}, f32[3072]{0:T(1024)S(1)}, f32[768]{0:T(1024)S(1)}, /*index=5*/f32[7...) all-reduce(f32[768]{0:T(1024)S(1)} %reduce_sum.194, ...), channel_id=8, replica_groups=mesh['seq'=4,'shard'=8] {'seq','shard'}, use_global_device_ids=true, to_apply=%region_27.28.clone | all-reduce | flops 9216 | bytes 73728
  810.4 29.3 %reduce-scatter.23.cloned.1.call-done = f32[24,768]{1,0:T(8,128)} async-done(((f32[768,768]{1,0:T(8,128)}), f32[24,768]{1,0:T(8,128)}) %reduce-scatter.23.cloned.1.call-update) | async-done | bytes 73744
  839.7 104.4 %reduce-scatter.19.cloned.1.call-done = f32[24,768]{1,0:T(8,128)} async-done(((f32[768,768]{1,0:T(8,128)}), f32[24,768]{1,0:T(8,128)}) %reduce-scatter.19.cloned.1.call-update) | async-done | bytes 73744
  944.1 141.7 %reduce-scatter.15.cloned.1.call-done = f32[24,3072]{1,0:T(8,128)} async-done(((f32[768,3072]{1,0:T(8,128)}), f32[24,3072]{1,0:T(8,128)}) %reduce-scatter.15.cloned.1.call-update) | async-done | bytes 294928 | tf_op jit(solution)/shard_map/reduce_scatter | solution.py:310
  1085.8 141.5 %reduce-scatter.17.cloned.1.call-done = f32[96,768]{1,0:T(8,128)} async-done(((f32[3072,768]{1,0:T(8,128)}), f32[96,768]{1,0:T(8,128)}) %reduce-scatter.17.cloned.1.call-update) | async-done | bytes 294928 | tf_op jit(solution)/shard_map/reduce_scatter | solution.py:311
  (524 shorter events, 491.1 us)
Async XLA Ops:
  7.2 61.3 %all-gather.11.cloned.1.call-start = ((), (), s32[]{:S(2)}) async-start(), calls=%async_computation.16 | async-start | bytes 1216512 | tf_op jit(solution)/shard_map/all_gather | solution.py:172
  8.8 121.8 %all-gather.7.cloned.1.call-start = ((), (), s32[]{:S(2)}) async-start(), calls=%async_computation.14 | async-start | bytes 1216512 | tf_op jit(solution)/shard_map/all_gather | solution.py:170
  10.3 181.8 %all-gather.9.cloned.1.call-start = ((), (), s32[]{:S(2)}) async-start(), calls=%async_computation.15 | async-start | bytes 1216512 | tf_op jit(solution)/shard_map/all_gather | solution.py:171
  11.9 341.5 %all-gather.13.cloned.1.call-start = ((), (), s32[]{:S(2)}) async-start(), calls=%async_computation.17 | async-start | bytes 1216512 | tf_op jit(solution)/shard_map/all_gather | solution.py:173
  13.5 344.4 %all-gather.15.cloned.1.call-start = ((), (), s32[]{:S(2)}) async-start(), calls=%async_computation.18 | async-start | bytes 4866048 | tf_op jit(solution)/shard_map/all_gather | solution.py:174
  74.7 64.2 %all-to-all-start.2 = ((bf16[4,256,12,64]{1,0,3,2:T(4,128)(2,1)}), bf16[4,256,12,64]{1,0,3,2:T(4,128)(2,1)S(1)}, u32[]{:S(2)}, u32[]{:S(2)}) async-start(bf16[4,256,12,64]{1,0,3,2:T(4,128)(2,1)} %reshape.248), calls=%async_computation.2 | async-start | bytes 3145728 | tf_op jit(solution)/shard_map/all_to_all | solution.py:206
  138.9 64.1 %all-to-all-start = ((bf16[4,256,12,64]{1,0,3,2:T(4,128)(2,1)}), bf16[4,256,12,64]{1,0,3,2:T(4,128)(2,1)S(1)}, u32[]{:S(2)}, u32[]{:S(2)}) async-start(bf16[4,256,12,64]{1,0,3,2:T(4,128)(2,1)} %reshape.246), calls=%async_computation | async-start | bytes 3145728 | tf_op jit(solution)/shard_map/all_to_all | solution.py:202
  203.0 25.4 %all-to-all-start.1 = ((bf16[4,256,12,64]{1,0,3,2:T(4,128)(2,1)}), bf16[4,256,12,64]{1,0,3,2:T(4,128)(2,1)}, u32[]{:S(2)}, u32[]{:S(2)}) async-start(bf16[4,256,12,64]{1,0,3,2:T(4,128)(2,1)} %reshape.247), calls=%async_computation.1 | async-start | bytes 3145728 | tf_op jit(solution)/shard_map/all_to_all | solution.py:205
  207.3 177.4 %all-gather.17.cloned.1.call-start = ((), (), s32[]{:S(2)}) async-start(), calls=%async_computation.19 | async-start | bytes 4866048 | tf_op jit(solution)/shard_map/all_gather | solution.py:175
  318.3 24.6 %all-to-all-start.3 = ((bf16[4,2,98304]{2,1,0:T(2,128)(2,1)}), bf16[4,2,98304]{2,1,0:T(2,128)(2,1)}, u32[]{:S(2)}, u32[]{:S(2)}) async-start(bf16[4,2,98304]{2,1,0:T(2,128)(2,1)} %reshape.299), calls=%async_computation.3 | async-start | bytes 3145728 | tf_op jit(solution)/shard_map/all_to_all | solution.py:210
  323.0 97.3 %copy-start.27 = (f32[768]{0:T(1024)}, f32[768]{0:T(1024)S(1)}, u32[]{:S(2)}) copy-start(f32[768]{0:T(1024)S(1)} %convert_element_type.180) | copy-start | bytes 9220
  323.0 61.8 %copy-start.29 = (f32[768]{0:T(1024)}, f32[768]{0:T(1024)S(1)}, u32[]{:S(2)}) copy-start(f32[768]{0:T(1024)S(1)} %convert_element_type.182) | copy-start | bytes 9220
  357.3 63.0 %copy-start = (f32[1024,768]{1,0:T(8,128)}, f32[1024,768]{1,0:T(8,128)S(1)}, u32[]{:S(2)}) copy-start(f32[1024,768]{1,0:T(8,128)S(1)} %get-tuple-element.629) | copy-start | bytes 9437188
  357.4 63.0 %copy-start.22 = (f32[1024]{0:T(1024)}, f32[1024]{0:T(1024)S(1)}, u32[]{:S(2)}) copy-start(f32[1024]{0:T(1024)S(1)} %broadcast_multiply_fusion.4) | copy-start | bytes 12292
  357.9 62.5 %copy-start.25 = (f32[1024]{0:T(1024)}, f32[1024]{0:T(1024)S(1)}, u32[]{:S(2)}) copy-start(f32[1024]{0:T(1024)S(1)} %add_rsqrt_fusion.1) | copy-start | bytes 12292
  396.8 17.0 %slice-start = ((s8[4718592]{0:T(1024)(128)(4,1)}), s8[4194304]{0:T(1024)(128)(4,1)S(1)}, s32[]{:S(2)}) async-start(s8[4718592]{0:T(1024)(128)(4,1)} %bitcast.315), calls=%async_computation.26 | async-start | bytes 8388608
  399.7 14.1 %copy-start.16 = (f32[1024,768]{1,0:T(8,128)}, f32[1024,768]{1,0:T(8,128)S(1)}, u32[]{:S(2)}) copy-start(f32[1024,768]{1,0:T(8,128)S(1)} %get-tuple-element.612) | copy-start | bytes 9437188
  430.9 24.4 %all-to-all-start.4 = ((bf16[4,256,12,64]{1,0,3,2:T(4,128)(2,1)}), bf16[4,256,12,64]{1,0,3,2:T(4,128)(2,1)}, u32[]{:S(2)}, u32[]{:S(2)}) async-start(bf16[4,256,12,64]{1,0,3,2:T(4,128)(2,1)} %reshape.251), calls=%async_computation.4 | async-start | bytes 3145728 | tf_op jit(solution)/shard_map/all_to_all | solution.py:255
  435.3 375.2 %reduce-scatter.13.cloned.1.call-start = ((), (), s32[]{:S(2)}) async-start(), calls=%async_computation.20 | async-start | bytes 2433024 | tf_op jit(solution)/shard_map/reduce_scatter | solution.py:309
  439.6 370.8 %reduce-scatter.21.cloned.1.call-start = ((), (), s32[]{:S(2)}) async-start(), calls=%async_computation.24 | async-start | bytes 2433024
  633.9 205.9 %reduce-scatter.23.cloned.1.call-start = ((), (), s32[]{:S(2)}) async-start(), calls=%async_computation.25 | async-start | bytes 2433024
  679.6 264.5 %reduce-scatter.19.cloned.1.call-start = ((), (), s32[]{:S(2)}) async-start(), calls=%async_computation.23 | async-start | bytes 2433024
  727.8 358.0 %reduce-scatter.15.cloned.1.call-start = ((), (), s32[]{:S(2)}) async-start(), calls=%async_computation.21 | async-start | bytes 9732096 | tf_op jit(solution)/shard_map/reduce_scatter | solution.py:310
  738.6 488.7 %reduce-scatter.17.cloned.1.call-start = ((), (), s32[]{:S(2)}) async-start(), calls=%async_computation.22 | async-start | bytes 9732096 | tf_op jit(solution)/shard_map/reduce_scatter | solution.py:311
  (50 other events, 241.9 us)
Sparse Core Ops, SparseCore 0:
  11.6 56.8 all-gather.10
  72.0 58.4 all-gather.6
  134.2 57.9 all-gather.8
  195.6 53.8 all-gather.12
  252.9 62.6 all-gather.14
  319.1 65.6 all-gather.16
  441.9 99.3 reduce-scatter.12
  634.0 100.7 reduce-scatter.20
  740.6 99.0 reduce-scatter.22
  845.4 98.6 reduce-scatter.18
  950.6 135.1 reduce-scatter.14
  1092.1 135.1 reduce-scatter.16
